TPU v7x, 32 devices: a whole 2x2x4 slice. The times are simulated.
32 devices in a mesh: row: 8 (over y, x, core), col: 4 (over z).
Axes of the slice: x: 2, y: 2, z: 4, core: 2. Of those that a mesh axis runs over, the one named last changes fastest.
Arguments:
- pair_rep: bfloat16 [128, 128, 128], P(('row', 'col')), may hold values from -16 to 16
- tile_mask: int32 [1, 1], replicated, may hold values from 0 to 1, as said below
- chain_ids: int32 [128], replicated, may hold values from 0 to 3, never falling along the last dimension, each value on 1 to 64 neighbouring positions
- chain_bias: float32 [2, 4], replicated, may hold values from -6 to 6
- row_project: bfloat16 [128, 512], replicated, may hold values from -0.5 to 0.5
- row_bias_proj: bfloat16 [128, 4], replicated, may hold values from -36 to 36
- row_output: bfloat16 [128, 128], replicated, may hold values from -0.5 to 0.5
- col_project: bfloat16 [128, 512], replicated, may hold values from -0.5 to 0.5
- col_bias_proj: bfloat16 [128, 4], replicated, may hold values from -36 to 36
- col_output: bfloat16 [128, 128], replicated, may hold values from -0.5 to 0.5
- tri_left: bfloat16 [128, 256], replicated, may hold values from -0.5 to 0.5
- tri_right: bfloat16 [128, 256], replicated, may hold values from -0.5 to 0.5
- tri_gate: bfloat16 [128, 128], replicated, may hold values from -0.5 to 0.5
- tri_output: bfloat16 [128, 128], replicated, may hold values from -1.5 to 1.5
Outputs:
- pair_out: bfloat16 [128, 128, 128], P('row', 'col')
Inputs may be any that keep to these rules, and one draw needn't show every extreme that they name: `tile_mask`: every diagonal entry is 1. `chain_ids`: chain numbers never fall along the residues.
All inputs are finite; a program needn't handle non-finite values.
Results may differ from a plain program's by a relative error of at most 0.018.
Values may be sent and summed in bfloat16 or wider, within the bound.
No kernel may reach another device: no remote copies, remote signals or barrier semaphores. Data moves between devices by JAX's collectives and lax.ppermute only.
A program may use at most 64 MiB of HBM per device.

v0:
```python
import jax
import jax.numpy as jnp
from jax import lax
from jax.sharding import PartitionSpec as P


def layer_norm(values):
    values = values.astype(jnp.float32)
    center = values - jnp.mean(values, axis=-1, keepdims=True)
    spread = jnp.mean(center * center, axis=-1, keepdims=True)
    return center * lax.rsqrt(spread + 1e-05)


def tile_rows(positions, tile_table, length):
    tile_count = tile_table.shape[0]
    tile_width = length // tile_count
    onehot = (positions[:, None] // tile_width == jnp.arange(tile_count)[None, :]).astype(
        jnp.float32
    )
    picked = jnp.dot(onehot, tile_table.astype(jnp.float32))
    spread_out = jnp.broadcast_to(picked[:, :, None], (positions.shape[0], tile_count, tile_width))
    return spread_out.reshape(positions.shape[0], length) > 0.5


def tile_pairs(row_pos, col_pos, tile_table, length):
    tile_count = tile_table.shape[0]
    tile_width = length // tile_count
    row_hot = (row_pos[:, None] // tile_width == jnp.arange(tile_count)[None, :]).astype(
        jnp.float32
    )
    col_hot = (col_pos[:, None] // tile_width == jnp.arange(tile_count)[None, :]).astype(
        jnp.float32
    )
    return jnp.dot(jnp.dot(row_hot, tile_table.astype(jnp.float32)), col_hot.T)


def attend_lines(
    queries,
    key_rows,
    value_rows,
    gate_pre,
    bias_all,
    key_ok,
    chain_ids,
    chain_add,
    line_dim,
    flipped,
):
    length = queries.shape[1 - line_dim]
    head_count = queries.shape[2]
    head_size = queries.shape[3]
    width_all = head_count * head_size
    query_rows = min(128, length)
    blocks = length // query_rows
    scaling = head_size ** (-0.5)
    spec_q = "lqhd" if line_dim == 0 else "qlhd"
    spec_k = "lkhd" if line_dim == 0 else "klhd"
    usable = key_ok[:, None, None, :]
    if flipped:
        bias_all = bias_all.transpose(0, 2, 1)
    same_all = (chain_ids[:, None] == chain_ids[None, :]).astype(jnp.float32)
    bias_all = bias_all + chain_add[:, None, None] * same_all[None]

    def one_block(offset):
        query_block = lax.dynamic_slice_in_dim(queries, offset, query_rows, 1 - line_dim)
        scores = (
            jnp.einsum(
                f"{spec_q},{spec_k}->lhqk",
                query_block,
                key_rows,
                preferred_element_type=jnp.float32,
            )
            * scaling
        )
        bias_block = lax.dynamic_slice_in_dim(bias_all, offset, query_rows, 1)
        scores = scores + bias_block[None]
        scores = jnp.where(usable, scores, -1000000000.0)
        row_peak = jnp.max(scores, axis=-1, keepdims=True)
        weights = jnp.exp(scores - row_peak)
        attention = (weights / jnp.sum(weights, axis=-1, keepdims=True)).astype(jnp.bfloat16)
        mixed_rows = jnp.einsum(
            f"lhqk,{spec_k}->{spec_q}", attention, value_rows, preferred_element_type=jnp.float32
        )
        mixed_rows = mixed_rows.reshape(mixed_rows.shape[:2] + (width_all,))
        gate_block = lax.dynamic_slice_in_dim(gate_pre, offset, query_rows, 1 - line_dim)
        return (mixed_rows * jax.nn.sigmoid(gate_block)).astype(jnp.bfloat16)

    if blocks == 1:
        return one_block(0)
    outputs = lax.map(one_block, jnp.arange(blocks, dtype=jnp.int32) * query_rows)
    if line_dim == 0:
        outputs = outputs.transpose(1, 0, 2, 3)
    return outputs.reshape(gate_pre.shape[:2] + (width_all,))


def tri_acts(normed, weights, allowed):
    channels = normed.shape[-1]
    projected = jnp.dot(normed.reshape(-1, channels), weights, preferred_element_type=jnp.float32)
    projected = projected.reshape(normed.shape[0], normed.shape[1], 2 * channels)
    return (
        jax.nn.sigmoid(projected[..., channels:]) * projected[..., :channels] * allowed[..., None]
    ).astype(jnp.bfloat16)


def gather_lines(piece):
    device_count = lax.axis_size("row") * lax.axis_size("col")
    sent = jnp.broadcast_to(piece[None], (device_count,) + piece.shape)
    got = lax.all_to_all(sent, ("row", "col"), 0, 0, tiled=True)
    heads, rows_here, length = piece.shape
    return got.transpose(1, 0, 2, 3).reshape(heads, device_count * rows_here, length)


def shards(
    pair_rep,
    tile_mask,
    chain_ids,
    chain_bias,
    row_project,
    row_bias_proj,
    row_output,
    col_project,
    col_bias_proj,
    col_output,
    tri_left,
    tri_right,
    tri_gate,
    tri_output,
):
    n_row = lax.axis_size("row")
    n_col = lax.axis_size("col")
    device_count = n_row * n_col
    rows_here, length, channels = pair_rep.shape
    head_count = row_bias_proj.shape[1]
    head_size = channels // head_count
    row_index = lax.axis_index("row")
    col_index = lax.axis_index("col")
    device_index = row_index * n_col + col_index
    block_rows = length // n_row
    block_cols = length // n_col
    local_lines = device_index * rows_here + jnp.arange(rows_here, dtype=jnp.int32)
    local_cols = (
        col_index * block_cols + row_index * rows_here + jnp.arange(rows_here, dtype=jnp.int32)
    )
    normed = layer_norm(pair_rep).astype(jnp.bfloat16)
    flat_rows = normed.reshape(rows_here * length, channels)
    bias_rows = jnp.dot(flat_rows, row_bias_proj, preferred_element_type=jnp.float32)
    bias_rows = bias_rows.reshape(rows_here, length, head_count).transpose(2, 0, 1)
    bias_all = gather_lines(bias_rows)
    projected = jnp.dot(flat_rows, row_project, preferred_element_type=jnp.float32).reshape(
        rows_here, length, 4 * channels
    )
    qkv_rows = (
        projected[..., : 3 * channels]
        .astype(jnp.bfloat16)
        .reshape(rows_here, length, 3, head_count, head_size)
    )
    key_ok = tile_rows(local_lines, tile_mask, length)
    mixed_rows = attend_lines(
        qkv_rows[:, :, 0],
        qkv_rows[:, :, 1],
        qkv_rows[:, :, 2],
        projected[..., 3 * channels :],
        bias_all,
        key_ok,
        chain_ids,
        chain_bias[0],
        0,
        False,
    )
    update = jnp.dot(
        mixed_rows.reshape(-1, channels), row_output, preferred_element_type=jnp.float32
    ).reshape(rows_here, length, channels)
    first_pair = (pair_rep.astype(jnp.float32) + update).astype(jnp.bfloat16)
    normed_first = layer_norm(first_pair).astype(jnp.bfloat16)
    bias_next = jnp.dot(
        normed_first.reshape(-1, channels), col_bias_proj, preferred_element_type=jnp.float32
    )
    bias_next = bias_next.reshape(rows_here, length, head_count).transpose(2, 0, 1)
    lanes = 128
    pair_chunks = (
        first_pair.reshape(rows_here, n_col, n_row, rows_here, channels)
        .transpose(2, 1, 0, 3, 4)
        .reshape(device_count, rows_here * rows_here * channels // lanes, lanes)
    )
    bias_high = bias_next.astype(jnp.bfloat16)
    bias_low = (bias_next - bias_high.astype(jnp.float32)).astype(jnp.bfloat16)
    bias_words = jnp.stack([bias_high, bias_low], axis=0).reshape(1, -1, lanes)
    bias_chunks = jnp.broadcast_to(bias_words, (device_count,) + bias_words.shape[1:])
    merged = lax.all_to_all(
        jnp.concatenate([pair_chunks, bias_chunks], axis=1), ("row", "col"), 0, 0, tiled=True
    )
    pair_rows = pair_chunks.shape[1]
    columns = (
        merged[:, :pair_rows]
        .reshape(device_count, rows_here, rows_here, channels)
        .transpose(2, 0, 1, 3)
        .reshape(rows_here, length, channels)
    )
    bias_got = (
        merged[:, pair_rows:]
        .reshape(device_count, 2, head_count, rows_here, length)
        .astype(jnp.float32)
    )
    bias_cols = (
        (bias_got[:, 0] + bias_got[:, 1]).transpose(1, 0, 2, 3).reshape(head_count, length, length)
    )
    normed_cols = layer_norm(columns).astype(jnp.bfloat16)
    projected_cols = jnp.dot(
        normed_cols.reshape(-1, channels), col_project, preferred_element_type=jnp.float32
    ).reshape(rows_here, length, 4 * channels)
    qkv_cols = (
        projected_cols[..., : 3 * channels]
        .astype(jnp.bfloat16)
        .reshape(rows_here, length, 3, head_count, head_size)
    )
    col_ok = tile_rows(local_cols, tile_mask.T, length)
    mixed_cols = attend_lines(
        qkv_cols[:, :, 0],
        qkv_cols[:, :, 1],
        qkv_cols[:, :, 2],
        projected_cols[..., 3 * channels :],
        bias_cols,
        col_ok,
        chain_ids,
        chain_bias[1],
        0,
        True,
    )
    update_cols = jnp.dot(
        mixed_cols.reshape(-1, channels), col_output, preferred_element_type=jnp.float32
    ).reshape(rows_here, length, channels)
    second_pair = (columns.astype(jnp.float32) + update_cols).astype(jnp.bfloat16)
    normed_second = layer_norm(second_pair).astype(jnp.bfloat16)
    edge_mask = tile_pairs(local_cols, jnp.arange(length, dtype=jnp.int32), tile_mask.T, length)
    both = jnp.dot(
        normed_second.reshape(-1, channels),
        jnp.concatenate([tri_left, tri_right], axis=1),
        preferred_element_type=jnp.float32,
    ).reshape(normed_second.shape[:2] + (4 * channels,))
    left_all, right_all = (
        (jax.nn.sigmoid(half[..., channels:]) * half[..., :channels] * edge_mask[..., None]).astype(
            jnp.bfloat16
        )
        for half in (both[..., : 2 * channels], both[..., 2 * channels :])
    )
    channels_here = channels // device_count
    edges = jnp.stack([left_all, right_all], axis=0).transpose(3, 0, 1, 2)
    edges_got = lax.all_to_all(edges, ("row", "col"), 0, 2, tiled=True)
    product_part = jnp.einsum(
        "cki,ckj->cij", edges_got[:, 0], edges_got[:, 1], preferred_element_type=jnp.float32
    )
    product_sent = (
        product_part.reshape(channels_here, n_row, block_rows, n_col, block_cols)
        .transpose(1, 3, 0, 2, 4)
        .reshape(device_count, channels_here, block_rows, block_cols)
    )
    raw_chunks = second_pair.reshape(rows_here, n_row, block_rows, channels).transpose(1, 2, 0, 3)
    early = n_row // 2
    raw_pieces = [lax.dynamic_index_in_dim(raw_chunks, row_index, 0, keepdims=False)]
    for shift in range(1, n_row):
        if shift == early + 1:
            product_sent, raw_chunks = lax.optimization_barrier((product_sent, raw_chunks))
        piece = lax.dynamic_index_in_dim(raw_chunks, (row_index + shift) % n_row, 0, keepdims=False)
        raw_pieces.append(
            lax.ppermute(piece, "row", perm=[(r, (r + shift) % n_row) for r in range(n_row)])
        )
    sources = (row_index - jnp.arange(n_row, dtype=jnp.int32)) % n_row
    raw_got = jnp.take(jnp.stack(raw_pieces, axis=0), sources, axis=0)
    own_pair = raw_got.transpose(1, 0, 2, 3).reshape(block_rows, block_cols, channels)
    product_got = lax.all_to_all(
        product_sent.reshape(device_count, -1, lanes), ("row", "col"), 0, 0, tiled=True
    )
    product_sum = product_got.reshape(channels, block_rows, block_cols).transpose(1, 2, 0)
    normed_own = layer_norm(own_pair).astype(jnp.bfloat16)
    gate_values = jax.nn.sigmoid(
        jnp.dot(normed_own.reshape(-1, channels), tri_gate, preferred_element_type=jnp.float32)
    ).reshape(block_rows, block_cols, channels)
    centered = layer_norm(product_sum).astype(jnp.bfloat16)
    update_tri = jnp.dot(
        centered.reshape(-1, channels), tri_output, preferred_element_type=jnp.float32
    ).reshape(block_rows, block_cols, channels)
    return (own_pair.astype(jnp.float32) + gate_values * update_tri).astype(jnp.bfloat16)


def solution(mesh):
    return jax.shard_map(
        shards,
        mesh=mesh,
        in_specs=(
            P(("row", "col"), None, None),
            P(),
            P(),
            P(),
            P(),
            P(),
            P(),
            P(),
            P(),
            P(),
            P(),
            P(),
            P(),
            P(),
        ),
        out_specs=P("row", "col", None),
        check_vma=False,
    )
```

profile of v0, /device:TPU:0, one launch (start us, length us, event | category | flops | bytes accessed | tf_op | source)
XLA Modules:
  0.0 80.6 jit_solution(5535929860434226173)
XLA Ops:
  0.0 1.1 %convert_reduce_fusion = f32[4,128]{1,0:T(4,128)S(1)} fusion(bf16[4,128,128]{2,1,0:T(8,128)(2,1)} %param.14), kind=kLoop, calls=%fused_computation.39 | loop fusion | flops 130560 | bytes 133120 | tf_op jit(solution)/shard_map/reduce_sum | solution.py:9
  1.4 0.7 copy-done.13
  2.4 0.7 broadcast_in_dim.33
  3.1 7.3 %all-to-all-start = ((f32[32,4,4,128]{3,2,1,0:T(4,128)}), f32[32,4,4,128]{3,2,1,0:T(4,128)S(1)}, u32[]{:S(2)}, u32[]{:S(2)}) async-start(f32[32,4,4,128]{3,2,1,0:T(4,128)} %broadcast_in_dim.33), calls=%async_computation | async-start | bytes 524288 | tf_op jit(solution)/shard_map/all_to_all | solution.py:108
  12.4 0.6 copy-done.8
  13.2 7.5 %all-to-all-done = f32[32,4,4,128]{3,2,1,0:T(4,128)S(1)} async-done(((f32[32,4,4,128]{3,2,1,0:T(4,128)}), f32[32,4,4,128]{3,2,1,0:T(4,128)S(1)}, u32[]{:S(2)}, u32[]{:S(2)}) %all-to-all-start) | async-done | bytes 262176 | tf_op jit(solution)/shard_map/all_to_all | solution.py:108
  23.6 0.7 copy-done.14
  24.7 0.8 pad_maximum_fusion
  25.4 2.7 %all-to-all-start.1 = ((bf16[32,48,128]{2,1,0:T(8,128)(2,1)}), bf16[32,48,128]{2,1,0:T(8,128)(2,1)S(1)}, u32[]{:S(2)}, u32[]{:S(2)}) async-start(bf16[32,48,128]{2,1,0:T(8,128)(2,1)} %pad_maximum_fusion), calls=%async_computation.1 | async-start | bytes 786432 | tf_op jit(solution)/shard_map/all_to_all | solution.py:189
  28.4 11.6 %all-to-all-done.1 = bf16[32,48,128]{2,1,0:T(8,128)(2,1)S(1)} async-done(((bf16[32,48,128]{2,1,0:T(8,128)(2,1)}), bf16[32,48,128]{2,1,0:T(8,128)(2,1)S(1)}, u32[]{:S(2)}, u32[]{:S(2)}) %all-to-all-start.1) | async-done | bytes 393248 | tf_op jit(solution)/shard_map/all_to_all | solution.py:189
  44.6 0.8 %copy-done.3 = f32[4,32,4,128]{3,2,1,0:T(4,128)S(1)} copy-done((f32[4,32,4,128]{3,2,1,0:T(4,128)S(1)}, f32[4,32,4,128]{3,2,1,0:T(4,128)}, u32[]{:S(2)}) %copy-start.3) | copy-done | bytes 262168
  47.2 0.9 %copy.168 = bf16[128,2,4,128]{3,2,1,0:T(4,128)(2,1)} copy(bf16[128,2,4,128]{0,3,2,1:T(8,128)(2,1)S(1)} %maximum_bitcast_fusion) | data formatting | bytes 524288 | tf_op jit(solution)/shard_map/transpose | solution.py:247
  48.0 3.8 %all-to-all-start.2 = ((bf16[128,2,4,128]{3,2,1,0:T(4,128)(2,1)}), bf16[128,2,4,128]{3,2,1,0:T(4,128)(2,1)S(1)}, u32[]{:S(2)}, u32[]{:S(2)}) async-start(bf16[128,2,4,128]{3,2,1,0:T(4,128)(2,1)} %copy.168), calls=%async_computation.2 | async-start | bytes 524288 | tf_op jit(solution)/shard_map/all_to_all | solution.py:248
  52.2 1.6 %collective-permute-start.1 = (bf16[16,4,128]{2,0,1:T(8,128)(2,1)S(1)}, bf16[16,4,128]{2,0,1:T(8,128)(2,1)S(1)}, u32[]{:S(2)}, u32[]{:S(2)}) collective-permute-start(bf16[16,4,128]{2,0,1:T(8,128)(2,1)S(1)} %get-tuple-element.18), channel_id=1, source_target_pairs={{0,8},{4,12},{8,16},{12,20},{16,24},{20,28},{24,0},{28,4},{1,9},{5... | collective-permute-start | bytes 49160 | tf_op jit(solution)/shard_map/ppermute | solution.py:265
  53.8 2.3 %collective-permute-start.2 = (bf16[16,4,128]{2,0,1:T(8,128)(2,1)S(1)}, bf16[16,4,128]{2,0,1:T(8,128)(2,1)S(1)}, u32[]{:S(2)}, u32[]{:S(2)}) collective-permute-start(bf16[16,4,128]{2,0,1:T(8,128)(2,1)S(1)} %get-tuple-element.17), channel_id=1, source_target_pairs={{0,12},{4,16},{8,20},{12,24},{16,28},{20,0},{24,4},{28,8},{1,13},{... | collective-permute-start | bytes 49160 | tf_op jit(solution)/shard_map/ppermute | solution.py:265
  57.0 0.8 %collective-permute-done.2 = bf16[16,4,128]{2,0,1:T(8,128)(2,1)S(1)} collective-permute-done((bf16[16,4,128]{2,0,1:T(8,128)(2,1)S(1)}, bf16[16,4,128]{2,0,1:T(8,128)(2,1)S(1)}, u32[]{:S(2)}, u32[]{:S(2)}) %collective-permute-start.2) | collective-permute-done | bytes 16416 | tf_op jit(solution)/shard_map/ppermute | solution.py:265
  57.8 4.3 %all-to-all-done.2 = bf16[128,2,4,128]{3,2,1,0:T(4,128)(2,1)S(1)} async-done(((bf16[128,2,4,128]{3,2,1,0:T(4,128)(2,1)}), bf16[128,2,4,128]{3,2,1,0:T(4,128)(2,1)S(1)}, u32[]{:S(2)}, u32[]{:S(2)}) %all-to-all-start.2) | async-done | bytes 262176 | tf_op jit(solution)/shard_map/all_to_all | solution.py:248
  63.2 0.9 %collective-permute-start.4 = (bf16[16,4,128]{2,0,1:T(8,128)(2,1)S(1)}, bf16[16,4,128]{2,0,1:T(8,128)(2,1)S(1)}, u32[]{:S(2)}, u32[]{:S(2)}) collective-permute-start(bf16[16,4,128]{2,0,1:T(8,128)(2,1)S(1)} %get-tuple-element.15), channel_id=1, source_target_pairs={{0,20},{4,24},{8,28},{12,0},{16,4},{20,8},{24,12},{28,16},{1,21},{... | collective-permute-start | bytes 49160 | tf_op jit(solution)/shard_map/ppermute | solution.py:265
  64.1 1.0 %reshape.442 = f32[32,16,128]{2,1,0:T(8,128)} reshape(f32[32,4,16,32]{3,2,1,0:T(8,128)S(1)} %bitcast.218) | data formatting | bytes 524288 | tf_op jit(solution)/shard_map/reshape | solution.py:271
  65.1 3.0 %all-to-all-start.3 = ((f32[32,16,128]{2,1,0:T(8,128)}), f32[32,16,128]{2,1,0:T(8,128)S(1)}, u32[]{:S(2)}, u32[]{:S(2)}) async-start(f32[32,16,128]{2,1,0:T(8,128)} %reshape.442), calls=%async_computation.3 | async-start | bytes 524288 | tf_op jit(solution)/shard_map/all_to_all | solution.py:270
  68.1 2.7 %collective-permute-start.5 = (bf16[16,4,128]{2,0,1:T(8,128)(2,1)S(1)}, bf16[16,4,128]{2,0,1:T(8,128)(2,1)S(1)}, u32[]{:S(2)}, u32[]{:S(2)}) collective-permute-start(bf16[16,4,128]{2,0,1:T(8,128)(2,1)S(1)} %get-tuple-element.14), channel_id=1, source_target_pairs={{0,24},{4,28},{8,0},{12,4},{16,8},{20,12},{24,16},{28,20},{1,25},{... | collective-permute-start | bytes 49160 | tf_op jit(solution)/shard_map/ppermute | solution.py:265
  70.8 1.4 %collective-permute-done.5 = bf16[16,4,128]{2,0,1:T(8,128)(2,1)S(1)} collective-permute-done((bf16[16,4,128]{2,0,1:T(8,128)(2,1)S(1)}, bf16[16,4,128]{2,0,1:T(8,128)(2,1)S(1)}, u32[]{:S(2)}, u32[]{:S(2)}) %collective-permute-start.5) | collective-permute-done | bytes 16416 | tf_op jit(solution)/shard_map/ppermute | solution.py:265
  75.2 3.1 %all-to-all-done.3 = f32[32,16,128]{2,1,0:T(8,128)S(1)} async-done(((f32[32,16,128]{2,1,0:T(8,128)}), f32[32,16,128]{2,1,0:T(8,128)S(1)}, u32[]{:S(2)}, u32[]{:S(2)}) %all-to-all-start.3) | async-done | bytes 262176 | tf_op jit(solution)/shard_map/all_to_all | solution.py:270
  79.7 1.0 %fusion.16 = bf16[16,32,128]{2,1,0:T(8,128)(2,1)} fusion(f32[16,32,128]{2,1,0:T(8,128)S(1)} %bitcast.231, f32[16,32,128]{2,1,0:T(8,128)S(1)} %bitcast.242, bf16[16,32,128]{1,0,2:T(8,128)(2,1)S(1)} %multiply_convert_fusion, bf16[128,128]{1,0:T(8,128)(2,1)S(1)} %copy-done.7), kind=kOutput, calls=%fused_computation.23 | convolution fusion | flops 16973824 | bytes 819200 | tf_op jit(solution)/shard_map/dot_general | solution.py:279
  (133 shorter events, 18.1 us)
Async XLA Ops:
  0.0 11.1 %copy-start = (bf16[128,512]{1,0:T(8,128)(2,1)S(1)}, bf16[128,512]{1,0:T(8,128)(2,1)}, u32[]{:S(2)}) copy-start(bf16[128,512]{1,0:T(8,128)(2,1)} %param.18) | copy-start | bytes 393220
  0.0 1.1 %copy-start.1 = (bf16[4,128,128]{2,1,0:T(8,128)(2,1)S(1)}, bf16[4,128,128]{2,1,0:T(8,128)(2,1)}, u32[]{:S(2)}) copy-start(bf16[4,128,128]{2,1,0:T(8,128)(2,1)} %param.14) | copy-start | bytes 393220
  1.4 0.7 copy-start.13
  3.1 17.6 %all-to-all-start = ((f32[32,4,4,128]{3,2,1,0:T(4,128)}), f32[32,4,4,128]{3,2,1,0:T(4,128)S(1)}, u32[]{:S(2)}, u32[]{:S(2)}) async-start(f32[32,4,4,128]{3,2,1,0:T(4,128)} %broadcast_in_dim.33), calls=%async_computation | async-start | bytes 524288 | tf_op jit(solution)/shard_map/all_to_all | solution.py:108
  22.2 0.8 copy-start.10
  23.5 0.7 copy-start.14
  25.4 14.5 %all-to-all-start.1 = ((bf16[32,48,128]{2,1,0:T(8,128)(2,1)}), bf16[32,48,128]{2,1,0:T(8,128)(2,1)S(1)}, u32[]{:S(2)}, u32[]{:S(2)}) async-start(bf16[32,48,128]{2,1,0:T(8,128)(2,1)} %pad_maximum_fusion), calls=%async_computation.1 | async-start | bytes 786432 | tf_op jit(solution)/shard_map/all_to_all | solution.py:189
  40.8 0.9 %copy-start.4 = (bf16[128,512]{1,0:T(8,128)(2,1)S(1)}, bf16[128,512]{1,0:T(8,128)(2,1)}, u32[]{:S(2)}) copy-start(bf16[128,512]{1,0:T(8,128)(2,1)} %param.21) | copy-start | bytes 393220
  41.0 0.7 copy-start.2
  44.4 1.0 %copy-start.3 = (f32[4,32,4,128]{3,2,1,0:T(4,128)S(1)}, f32[4,32,4,128]{3,2,1,0:T(4,128)}, u32[]{:S(2)}) copy-start(f32[4,32,4,128]{3,2,1,0:T(4,128)} %copy-done.2) | copy-start | bytes 786436
  44.4 1.0 %copy-start.11 = (bf16[128,128]{1,0:T(8,128)(2,1)S(1)}, bf16[128,128]{1,0:T(8,128)(2,1)}, u32[]{:S(2)}) copy-start(bf16[128,128]{1,0:T(8,128)(2,1)} %param.23) | copy-start | bytes 98308
  45.7 0.8 %copy-start.5 = (bf16[128,256]{1,0:T(8,128)(2,1)S(1)}, bf16[128,256]{1,0:T(8,128)(2,1)}, u32[]{:S(2)}) copy-start(bf16[128,256]{1,0:T(8,128)(2,1)} %param.25) | copy-start | bytes 196612
  45.7 0.9 %copy-start.6 = (bf16[128,256]{1,0:T(8,128)(2,1)S(1)}, bf16[128,256]{1,0:T(8,128)(2,1)}, u32[]{:S(2)}) copy-start(bf16[128,256]{1,0:T(8,128)(2,1)} %param.24) | copy-start | bytes 196612
  48.0 14.1 %all-to-all-start.2 = ((bf16[128,2,4,128]{3,2,1,0:T(4,128)(2,1)}), bf16[128,2,4,128]{3,2,1,0:T(4,128)(2,1)S(1)}, u32[]{:S(2)}, u32[]{:S(2)}) async-start(bf16[128,2,4,128]{3,2,1,0:T(4,128)(2,1)} %copy.168), calls=%async_computation.2 | async-start | bytes 524288 | tf_op jit(solution)/shard_map/all_to_all | solution.py:248
  51.9 4.8 %collective-permute-start = (bf16[16,4,128]{2,0,1:T(8,128)(2,1)S(1)}, bf16[16,4,128]{2,0,1:T(8,128)(2,1)S(1)}, u32[]{:S(2)}, u32[]{:S(2)}) collective-permute-start(bf16[16,4,128]{2,0,1:T(8,128)(2,1)S(1)} %get-tuple-element.19), channel_id=1, source_target_pairs={{0,4},{4,8},{8,12},{12,16},{16,20},{20,24},{24,28},{28,0},{1,5},{5... | collective-permute-start | bytes 49160 | tf_op jit(solution)/shard_map/ppermute | solution.py:265
  52.2 4.8 %collective-permute-start.1 = (bf16[16,4,128]{2,0,1:T(8,128)(2,1)S(1)}, bf16[16,4,128]{2,0,1:T(8,128)(2,1)S(1)}, u32[]{:S(2)}, u32[]{:S(2)}) collective-permute-start(bf16[16,4,128]{2,0,1:T(8,128)(2,1)S(1)} %get-tuple-element.18), channel_id=1, source_target_pairs={{0,8},{4,12},{8,16},{12,20},{16,24},{20,28},{24,0},{28,4},{1,9},{5... | collective-permute-start | bytes 49160 | tf_op jit(solution)/shard_map/ppermute | solution.py:265
  53.8 4.0 %collective-permute-start.2 = (bf16[16,4,128]{2,0,1:T(8,128)(2,1)S(1)}, bf16[16,4,128]{2,0,1:T(8,128)(2,1)S(1)}, u32[]{:S(2)}, u32[]{:S(2)}) collective-permute-start(bf16[16,4,128]{2,0,1:T(8,128)(2,1)S(1)} %get-tuple-element.17), channel_id=1, source_target_pairs={{0,12},{4,16},{8,20},{12,24},{16,28},{20,0},{24,4},{28,8},{1,13},{... | collective-permute-start | bytes 49160 | tf_op jit(solution)/shard_map/ppermute | solution.py:265
  56.1 8.0 %collective-permute-start.3 = (bf16[16,4,128]{2,0,1:T(8,128)(2,1)S(1)}, bf16[16,4,128]{2,0,1:T(8,128)(2,1)S(1)}, u32[]{:S(2)}, u32[]{:S(2)}) collective-permute-start(bf16[16,4,128]{2,0,1:T(8,128)(2,1)S(1)} %get-tuple-element.16), channel_id=1, source_target_pairs={{0,16},{4,20},{8,24},{12,28},{16,0},{20,4},{24,8},{28,12},{1,17},{... | collective-permute-start | bytes 49160 | tf_op jit(solution)/shard_map/ppermute | solution.py:265
  63.2 7.6 %collective-permute-start.4 = (bf16[16,4,128]{2,0,1:T(8,128)(2,1)S(1)}, bf16[16,4,128]{2,0,1:T(8,128)(2,1)S(1)}, u32[]{:S(2)}, u32[]{:S(2)}) collective-permute-start(bf16[16,4,128]{2,0,1:T(8,128)(2,1)S(1)} %get-tuple-element.15), channel_id=1, source_target_pairs={{0,20},{4,24},{8,28},{12,0},{16,4},{20,8},{24,12},{28,16},{1,21},{... | collective-permute-start | bytes 49160 | tf_op jit(solution)/shard_map/ppermute | solution.py:265
  65.1 13.2 %all-to-all-start.3 = ((f32[32,16,128]{2,1,0:T(8,128)}), f32[32,16,128]{2,1,0:T(8,128)S(1)}, u32[]{:S(2)}, u32[]{:S(2)}) async-start(f32[32,16,128]{2,1,0:T(8,128)} %reshape.442), calls=%async_computation.3 | async-start | bytes 524288 | tf_op jit(solution)/shard_map/all_to_all | solution.py:270
  68.1 4.2 %collective-permute-start.5 = (bf16[16,4,128]{2,0,1:T(8,128)(2,1)S(1)}, bf16[16,4,128]{2,0,1:T(8,128)(2,1)S(1)}, u32[]{:S(2)}, u32[]{:S(2)}) collective-permute-start(bf16[16,4,128]{2,0,1:T(8,128)(2,1)S(1)} %get-tuple-element.14), channel_id=1, source_target_pairs={{0,24},{4,28},{8,0},{12,4},{16,8},{20,12},{24,16},{28,20},{1,25},{... | collective-permute-start | bytes 49160 | tf_op jit(solution)/shard_map/ppermute | solution.py:265
  70.8 1.6 %collective-permute-start.6 = (bf16[16,4,128]{2,0,1:T(8,128)(2,1)S(1)}, bf16[16,4,128]{2,0,1:T(8,128)(2,1)S(1)}, u32[]{:S(2)}, u32[]{:S(2)}) collective-permute-start(bf16[16,4,128]{2,0,1:T(8,128)(2,1)S(1)} %get-tuple-element.13), channel_id=1, source_target_pairs={{0,28},{4,0},{8,4},{12,8},{16,12},{20,16},{24,20},{28,24},{1,29},{... | collective-permute-start | bytes 49160 | tf_op jit(solution)/shard_map/ppermute | solution.py:265
  74.1 0.8 copy-start.12
  78.9 0.8 copy-start.7
  (2 other events, 1.3 us)
where the time goes:
time: 81.4 us; the launch traced here: 80.6 us
  waiting for transfers between devices  29.2 us (36%)
  starting transfers between devices  25.2 us (31%)
  local copies, waits for them, and re-layouts  13.8 us (17%)
  matrix products  6.34 us (8%)
  other arithmetic  4.88 us (6%)
  between operations  1.33 us (2%)
    all_to_all x1, waiting for transfers between devices, shards(): lax.all_to_all(jnp.concatenate([pair_chunks, bias_chunks], axis=1), ('row...  11.6 us
    ppermute x7, starting transfers between devices, shards(): lax.ppermute(piece, 'row', perm=[(r, (r + shift) % n_row) for r in range(...  8.38 us
    all_to_all x1, waiting for transfers between devices, gather_lines(): got = lax.all_to_all(sent, ('row', 'col'), 0, 0, tiled=True)  7.48 us
    all_to_all x1, starting transfers between devices, gather_lines(): got = lax.all_to_all(sent, ('row', 'col'), 0, 0, tiled=True)  7.33 us
    unnamed x38, local copies, waits for them, and re-layouts  6.73 us
    all_to_all x1, waiting for transfers between devices, shards(): edges_got = lax.all_to_all(edges, ('row', 'col'), 0, 2, tiled=True)  4.28 us
    all_to_all x1, starting transfers between devices, shards(): edges_got = lax.all_to_all(edges, ('row', 'col'), 0, 2, tiled=True)  3.82 us
    all_to_all x1, waiting for transfers between devices, shards(): lax.all_to_all(product_sent.reshape(device_count, -1, lanes), ('row', 'co...  3.08 us
  transfers between devices with their start and end apart: 11, of which 8 were waited for; matrix products, arithmetic and copies ran while one was open for 6% of the time, Pallas kernels for 0%

commit v1 on v0

--- a/solution.py
+++ b/solution.py
@@ -245,7 +245,12 @@
     )
     channels_here = channels // device_count
     edges = jnp.stack([left_all, right_all], axis=0).transpose(3, 0, 1, 2)
-    edges_got = lax.all_to_all(edges, ("row", "col"), 0, 2, tiled=True)
+    edges_got = jnp.concatenate(
+        lax.all_to_all(
+            jnp.stack(jnp.split(edges, lax.axis_size(("row", "col")), axis=0)), ("row", "col"), 0, 0
+        ),
+        axis=2,
+    )
     product_part = jnp.einsum(
         "cki,ckj->cij", edges_got[:, 0], edges_got[:, 1], preferred_element_type=jnp.float32
     )

time: 81.4 us -> 112 us (1.38)
  local copies, waits for them, and re-layouts: 13.8 us -> 41.6 us
  matrix products: 6.34 us -> 8.19 us
  other arithmetic: 4.88 us -> 6.52 us
    unnamed x38 -> x63, local copies, waits for them, and re-layouts: 6.73 us -> 26.9 us
    another operation x0 -> x2, local copies, waits for them, and re-layouts: none -> 7.89 us  [shards(): jnp.stack(jnp.split(edges, lax.axis_size(('row', 'col')), axis=0))]
  transfers between devices with their start and end apart: 11 -> 11, of which waited for: 8 -> 8; matrix products, arithmetic and copies ran while one was open for 6% -> 7% of each run, Pallas kernels for 0% -> 0%
where the time goes in v1:
time: 112 us
  local copies, waits for them, and re-layouts  41.6 us (37%)
  waiting for transfers between devices  28.5 us (25%)
  starting transfers between devices  25.3 us (23%)
  matrix products  8.19 us (7%)
  other arithmetic  6.52 us (6%)
  between operations  1.36 us (1%)
    unnamed x63, local copies, waits for them, and re-layouts  26.9 us
    all_to_all x1, waiting for transfers between devices, shards(): lax.all_to_all(jnp.concatenate([pair_chunks, bias_chunks], axis=1), ('row...  11.4 us
    ppermute x7, starting transfers between devices, shards(): lax.ppermute(piece, 'row', perm=[(r, (r + shift) % n_row) for r in range(...  8.38 us
    another operation x2, local copies, waits for them, and re-layouts, shards(): jnp.stack(jnp.split(edges, lax.axis_size(('row', 'col')), axis=0))  7.89 us
    all_to_all x1, starting transfers between devices, gather_lines(): got = lax.all_to_all(sent, ('row', 'col'), 0, 0, tiled=True)  7.33 us
    all_to_all x1, waiting for transfers between devices, gather_lines(): got = lax.all_to_all(sent, ('row', 'col'), 0, 0, tiled=True)  6.4 us
    all_to_all x1, waiting for transfers between devices, shards(): lax.all_to_all(jnp.stack(jnp.split(edges, lax.axis_size(('row', 'col')),...  4.28 us
    all_to_all x1, starting transfers between devices, shards(): lax.all_to_all(jnp.stack(jnp.split(edges, lax.axis_size(('row', 'col')),...  3.81 us
  transfers between devices with their start and end apart: 11, of which 8 were waited for; matrix products, arithmetic and copies ran while one was open for 7% of the time, Pallas kernels for 0%

profile of v1, /device:TPU:0, one launch (start us, length us, event | category | flops | bytes accessed | tf_op | source)
XLA Modules:
  0.0 111.5 jit_solution(16221252825036204550)
XLA Ops:
  0.0 1.1 convert_reduce_fusion
  1.1 1.1 %fusion.26 = f32[4,128]{1,0:T(4,128)S(1)} fusion(bf16[4,128,128]{2,1,0:T(8,128)(2,1)} %param.14, f32[4,128]{1,0:T(4,128)S(1)} %broadcast_multiply_fusion.5), kind=kLoop, calls=%fused_computation.50 | loop fusion | flops 261632 | bytes 135168 | tf_op jit(solution)/shard_map/reduce_sum | solution.py:10
  2.3 1.2 %convolution_bitcast_fusion.1 = f32[4,4,128]{2,0,1:T(4,128)S(1)} fusion(bf16[4,128,128]{2,1,0:T(8,128)(2,1)} %param.14, f32[4,128]{1,0:T(4,128)S(1)} %add_rsqrt_fusion.4, f32[4,128]{1,0:T(4,128)S(1)} %broadcast_multiply_fusion.5, bf16[128,4]{0,1:T(4,128)(2,1)} %param.19), kind=kOutput, calls=%fused_computation.25 | convolution fusion | flops 786432 | bytes 144384 | tf_op jit(solution)/shard_map/dot_general | solution.py:146
  4.2 7.3 %all-to-all-start = ((f32[32,4,4,128]{3,2,1,0:T(4,128)}), f32[32,4,4,128]{3,2,1,0:T(4,128)S(1)}, u32[]{:S(2)}, u32[]{:S(2)}) async-start(f32[32,4,4,128]{3,2,1,0:T(4,128)} %broadcast_in_dim.33), calls=%async_computation | async-start | bytes 524288 | tf_op jit(solution)/shard_map/all_to_all | solution.py:108
  12.2 1.3 %fusion.96 = f32[4,128,512]{2,1,0:T(8,128)S(1)} fusion(bf16[128,512]{1,0:T(8,128)(2,1)S(1)} %copy-done, bf16[4,128,128]{2,1,0:T(8,128)(2,1)} %param.14, f32[4,128]{1,0:T(4,128)S(1)} %add_rsqrt_fusion.4, f32[4,128]{1,0:T(4,128)S(1)} %broadcast_multiply_fusion.5), kind=kOutput, calls=%fused_computation.174 | convolution fusion | flops 67371008 | bytes 1314816 | tf_op jit(solution)/shard_map/dot_general | solution.py:149
  15.4 6.4 %all-to-all-done = f32[32,4,4,128]{3,2,1,0:T(4,128)S(1)} async-done(((f32[32,4,4,128]{3,2,1,0:T(4,128)}), f32[32,4,4,128]{3,2,1,0:T(4,128)S(1)}, u32[]{:S(2)}, u32[]{:S(2)}) %all-to-all-start) | async-done | bytes 262176 | tf_op jit(solution)/shard_map/all_to_all | solution.py:108
  25.3 2.8 %all-to-all-start.1 = ((bf16[32,48,128]{2,1,0:T(8,128)(2,1)}), bf16[32,48,128]{2,1,0:T(8,128)(2,1)S(1)}, u32[]{:S(2)}, u32[]{:S(2)}) async-start(bf16[32,48,128]{2,1,0:T(8,128)(2,1)} %pad_maximum_fusion), calls=%async_computation.1 | async-start | bytes 786432 | tf_op jit(solution)/shard_map/all_to_all | solution.py:189
  28.4 11.4 %all-to-all-done.1 = bf16[32,48,128]{2,1,0:T(8,128)(2,1)S(1)} async-done(((bf16[32,48,128]{2,1,0:T(8,128)(2,1)}), bf16[32,48,128]{2,1,0:T(8,128)(2,1)S(1)}, u32[]{:S(2)}, u32[]{:S(2)}) %all-to-all-start.1) | async-done | bytes 393248 | tf_op jit(solution)/shard_map/all_to_all | solution.py:189
  48.9 0.9 fusion.59
  52.3 0.9 fusion.55
  61.6 0.9 fusion.44
  63.3 0.9 fusion.42
  72.6 7.0 %copy.239 = bf16[32,4,2,4,128]{4,3,2,1,0:T(4,128)(2,1)} copy(bf16[32,4,2,4,128]{1,4,3,2,0:T(8,128)(2,1)} %fusion.32) | data formatting | bytes 524288 | tf_op jit(solution)/shard_map/stack | solution.py:250
  79.7 3.8 %all-to-all-start.2 = ((bf16[32,4,2,4,128]{4,3,2,1,0:T(4,128)(2,1)}), bf16[32,4,2,4,128]{4,3,2,1,0:T(4,128)(2,1)S(1)}, u32[]{:S(2)}, u32[]{:S(2)}) async-start(bf16[32,4,2,4,128]{4,3,2,1,0:T(4,128)(2,1)} %copy.239), calls=%async_computation.2 | async-start | bytes 524288 | tf_op jit(solution)/shard_map/all_to_all | solution.py:249
  83.8 1.6 %collective-permute-start.1 = (bf16[16,4,128]{2,0,1:T(8,128)(2,1)S(1)}, bf16[16,4,128]{2,0,1:T(8,128)(2,1)S(1)}, u32[]{:S(2)}, u32[]{:S(2)}) collective-permute-start(bf16[16,4,128]{2,0,1:T(8,128)(2,1)S(1)} %get-tuple-element.18), channel_id=1, source_target_pairs={{0,8},{4,12},{8,16},{12,20},{16,24},{20,28},{24,0},{28,4},{1,9},{5... | collective-permute-start | bytes 49160 | tf_op jit(solution)/shard_map/ppermute | solution.py:270
  85.5 2.3 %collective-permute-start.2 = (bf16[16,4,128]{2,0,1:T(8,128)(2,1)S(1)}, bf16[16,4,128]{2,0,1:T(8,128)(2,1)S(1)}, u32[]{:S(2)}, u32[]{:S(2)}) collective-permute-start(bf16[16,4,128]{2,0,1:T(8,128)(2,1)S(1)} %get-tuple-element.17), channel_id=1, source_target_pairs={{0,12},{4,16},{8,20},{12,24},{16,28},{20,0},{24,4},{28,8},{1,13},{... | collective-permute-start | bytes 49160 | tf_op jit(solution)/shard_map/ppermute | solution.py:270
  89.4 4.3 %all-to-all-done.2 = bf16[32,4,2,4,128]{4,3,2,1,0:T(4,128)(2,1)S(1)} async-done(((bf16[32,4,2,4,128]{4,3,2,1,0:T(4,128)(2,1)}), bf16[32,4,2,4,128]{4,3,2,1,0:T(4,128)(2,1)S(1)}, u32[]{:S(2)}, u32[]{:S(2)}) %all-to-all-start.2) | async-done | bytes 262176 | tf_op jit(solution)/shard_map/all_to_all | solution.py:249
  94.7 0.9 collective-permute-start.4
  95.6 1.0 reshape.450
  96.6 3.0 %all-to-all-start.3 = ((f32[32,16,128]{2,1,0:T(8,128)}), f32[32,16,128]{2,1,0:T(8,128)S(1)}, u32[]{:S(2)}, u32[]{:S(2)}) async-start(f32[32,16,128]{2,1,0:T(8,128)} %reshape.450), calls=%async_computation.3 | async-start | bytes 524288 | tf_op jit(solution)/shard_map/all_to_all | solution.py:275
  99.5 2.7 %collective-permute-start.5 = (bf16[16,4,128]{2,0,1:T(8,128)(2,1)S(1)}, bf16[16,4,128]{2,0,1:T(8,128)(2,1)S(1)}, u32[]{:S(2)}, u32[]{:S(2)}) collective-permute-start(bf16[16,4,128]{2,0,1:T(8,128)(2,1)S(1)} %get-tuple-element.14), channel_id=1, source_target_pairs={{0,24},{4,28},{8,0},{12,4},{16,8},{20,12},{24,16},{28,20},{1,25},{... | collective-permute-start | bytes 49160 | tf_op jit(solution)/shard_map/ppermute | solution.py:270
  102.3 1.4 %collective-permute-done.5 = bf16[16,4,128]{2,0,1:T(8,128)(2,1)S(1)} collective-permute-done((bf16[16,4,128]{2,0,1:T(8,128)(2,1)S(1)}, bf16[16,4,128]{2,0,1:T(8,128)(2,1)S(1)}, u32[]{:S(2)}, u32[]{:S(2)}) %collective-permute-start.5) | collective-permute-done | bytes 16416 | tf_op jit(solution)/shard_map/ppermute | solution.py:270
  106.1 3.7 %all-to-all-done.3 = f32[32,16,128]{2,1,0:T(8,128)S(1)} async-done(((f32[32,16,128]{2,1,0:T(8,128)}), f32[32,16,128]{2,1,0:T(8,128)S(1)}, u32[]{:S(2)}, u32[]{:S(2)}) %all-to-all-start.3) | async-done | bytes 262176 | tf_op jit(solution)/shard_map/all_to_all | solution.py:275
  110.5 1.0 fusion.16
  (158 shorter events, 41.3 us)
Async XLA Ops:
  0.0 12.2 %copy-start = (bf16[128,512]{1,0:T(8,128)(2,1)S(1)}, bf16[128,512]{1,0:T(8,128)(2,1)}, u32[]{:S(2)}) copy-start(bf16[128,512]{1,0:T(8,128)(2,1)} %param.18) | copy-start | bytes 393220
  0.0 23.5 %copy-start.1 = (bf16[4,128,128]{2,1,0:T(8,128)(2,1)S(1)}, bf16[4,128,128]{2,1,0:T(8,128)(2,1)}, u32[]{:S(2)}) copy-start(bf16[4,128,128]{2,1,0:T(8,128)(2,1)} %param.14) | copy-start | bytes 393220
  0.0 23.5 %copy-start.8 = (bf16[128,128]{1,0:T(8,128)(2,1)S(1)}, bf16[128,128]{1,0:T(8,128)(2,1)}, u32[]{:S(2)}) copy-start(bf16[128,128]{1,0:T(8,128)(2,1)} %param.20) | copy-start | bytes 98308
  0.0 24.1 %copy-start.11 = (bf16[128,4]{0,1:T(4,128)(2,1)S(1)}, bf16[128,4]{0,1:T(4,128)(2,1)}, u32[]{:S(2)}) copy-start(bf16[128,4]{0,1:T(4,128)(2,1)} %param.22) | copy-start | bytes 3076
  4.2 17.6 %all-to-all-start = ((f32[32,4,4,128]{3,2,1,0:T(4,128)}), f32[32,4,4,128]{3,2,1,0:T(4,128)S(1)}, u32[]{:S(2)}, u32[]{:S(2)}) async-start(f32[32,4,4,128]{3,2,1,0:T(4,128)} %broadcast_in_dim.33), calls=%async_computation | async-start | bytes 524288 | tf_op jit(solution)/shard_map/all_to_all | solution.py:108
  14.6 27.0 %copy-start.4 = (bf16[128,512]{1,0:T(8,128)(2,1)S(1)}, bf16[128,512]{1,0:T(8,128)(2,1)}, u32[]{:S(2)}) copy-start(bf16[128,512]{1,0:T(8,128)(2,1)} %param.21) | copy-start | bytes 393220
  25.3 14.5 %all-to-all-start.1 = ((bf16[32,48,128]{2,1,0:T(8,128)(2,1)}), bf16[32,48,128]{2,1,0:T(8,128)(2,1)S(1)}, u32[]{:S(2)}, u32[]{:S(2)}) async-start(bf16[32,48,128]{2,1,0:T(8,128)(2,1)} %pad_maximum_fusion), calls=%async_computation.1 | async-start | bytes 786432 | tf_op jit(solution)/shard_map/all_to_all | solution.py:189
  40.9 0.7 copy-start.2
  41.0 3.5 %copy-start.9 = (bf16[128,128]{1,0:T(8,128)(2,1)S(1)}, bf16[128,128]{1,0:T(8,128)(2,1)}, u32[]{:S(2)}) copy-start(bf16[128,128]{1,0:T(8,128)(2,1)} %param.23) | copy-start | bytes 98308
  41.9 3.1 %copy-start.5 = (bf16[128,256]{1,0:T(8,128)(2,1)S(1)}, bf16[128,256]{1,0:T(8,128)(2,1)}, u32[]{:S(2)}) copy-start(bf16[128,256]{1,0:T(8,128)(2,1)} %param.25) | copy-start | bytes 196612
  41.9 3.1 %copy-start.6 = (bf16[128,256]{1,0:T(8,128)(2,1)S(1)}, bf16[128,256]{1,0:T(8,128)(2,1)}, u32[]{:S(2)}) copy-start(bf16[128,256]{1,0:T(8,128)(2,1)} %param.24) | copy-start | bytes 196612
  42.4 2.1 %copy-start.3 = (f32[4,32,4,128]{3,2,1,0:T(4,128)S(1)}, f32[4,32,4,128]{3,2,1,0:T(4,128)}, u32[]{:S(2)}) copy-start(f32[4,32,4,128]{3,2,1,0:T(4,128)} %copy-done.2) | copy-start | bytes 786436
  72.6 33.1 %copy-start.10 = (bf16[128,128]{1,0:T(8,128)(2,1)S(1)}, bf16[128,128]{1,0:T(8,128)(2,1)}, u32[]{:S(2)}) copy-start(bf16[128,128]{1,0:T(8,128)(2,1)} %param.26) | copy-start | bytes 98308
  79.7 30.9 %copy-start.7 = (bf16[128,128]{1,0:T(8,128)(2,1)S(1)}, bf16[128,128]{1,0:T(8,128)(2,1)}, u32[]{:S(2)}) copy-start(bf16[128,128]{1,0:T(8,128)(2,1)} %param.27) | copy-start | bytes 98308
  79.7 14.0 %all-to-all-start.2 = ((bf16[32,4,2,4,128]{4,3,2,1,0:T(4,128)(2,1)}), bf16[32,4,2,4,128]{4,3,2,1,0:T(4,128)(2,1)S(1)}, u32[]{:S(2)}, u32[]{:S(2)}) async-start(bf16[32,4,2,4,128]{4,3,2,1,0:T(4,128)(2,1)} %copy.239), calls=%async_computation.2 | async-start | bytes 524288 | tf_op jit(solution)/shard_map/all_to_all | solution.py:249
  83.5 4.8 %collective-permute-start = (bf16[16,4,128]{2,0,1:T(8,128)(2,1)S(1)}, bf16[16,4,128]{2,0,1:T(8,128)(2,1)S(1)}, u32[]{:S(2)}, u32[]{:S(2)}) collective-permute-start(bf16[16,4,128]{2,0,1:T(8,128)(2,1)S(1)} %get-tuple-element.19), channel_id=1, source_target_pairs={{0,4},{4,8},{8,12},{12,16},{16,20},{20,24},{24,28},{28,0},{1,5},{5... | collective-permute-start | bytes 49160 | tf_op jit(solution)/shard_map/ppermute | solution.py:270
  83.8 4.8 %collective-permute-start.1 = (bf16[16,4,128]{2,0,1:T(8,128)(2,1)S(1)}, bf16[16,4,128]{2,0,1:T(8,128)(2,1)S(1)}, u32[]{:S(2)}, u32[]{:S(2)}) collective-permute-start(bf16[16,4,128]{2,0,1:T(8,128)(2,1)S(1)} %get-tuple-element.18), channel_id=1, source_target_pairs={{0,8},{4,12},{8,16},{12,20},{16,24},{20,28},{24,0},{28,4},{1,9},{5... | collective-permute-start | bytes 49160 | tf_op jit(solution)/shard_map/ppermute | solution.py:270
  85.5 4.0 %collective-permute-start.2 = (bf16[16,4,128]{2,0,1:T(8,128)(2,1)S(1)}, bf16[16,4,128]{2,0,1:T(8,128)(2,1)S(1)}, u32[]{:S(2)}, u32[]{:S(2)}) collective-permute-start(bf16[16,4,128]{2,0,1:T(8,128)(2,1)S(1)} %get-tuple-element.17), channel_id=1, source_target_pairs={{0,12},{4,16},{8,20},{12,24},{16,28},{20,0},{24,4},{28,8},{1,13},{... | collective-permute-start | bytes 49160 | tf_op jit(solution)/shard_map/ppermute | solution.py:270
  87.7 7.9 %collective-permute-start.3 = (bf16[16,4,128]{2,0,1:T(8,128)(2,1)S(1)}, bf16[16,4,128]{2,0,1:T(8,128)(2,1)S(1)}, u32[]{:S(2)}, u32[]{:S(2)}) collective-permute-start(bf16[16,4,128]{2,0,1:T(8,128)(2,1)S(1)} %get-tuple-element.16), channel_id=1, source_target_pairs={{0,16},{4,20},{8,24},{12,28},{16,0},{20,4},{24,8},{28,12},{1,17},{... | collective-permute-start | bytes 49160 | tf_op jit(solution)/shard_map/ppermute | solution.py:270
  94.7 7.6 %collective-permute-start.4 = (bf16[16,4,128]{2,0,1:T(8,128)(2,1)S(1)}, bf16[16,4,128]{2,0,1:T(8,128)(2,1)S(1)}, u32[]{:S(2)}, u32[]{:S(2)}) collective-permute-start(bf16[16,4,128]{2,0,1:T(8,128)(2,1)S(1)} %get-tuple-element.15), channel_id=1, source_target_pairs={{0,20},{4,24},{8,28},{12,0},{16,4},{20,8},{24,12},{28,16},{1,21},{... | collective-permute-start | bytes 49160 | tf_op jit(solution)/shard_map/ppermute | solution.py:270
  96.6 13.2 %all-to-all-start.3 = ((f32[32,16,128]{2,1,0:T(8,128)}), f32[32,16,128]{2,1,0:T(8,128)S(1)}, u32[]{:S(2)}, u32[]{:S(2)}) async-start(f32[32,16,128]{2,1,0:T(8,128)} %reshape.450), calls=%async_computation.3 | async-start | bytes 524288 | tf_op jit(solution)/shard_map/all_to_all | solution.py:275
  99.5 4.2 %collective-permute-start.5 = (bf16[16,4,128]{2,0,1:T(8,128)(2,1)S(1)}, bf16[16,4,128]{2,0,1:T(8,128)(2,1)S(1)}, u32[]{:S(2)}, u32[]{:S(2)}) collective-permute-start(bf16[16,4,128]{2,0,1:T(8,128)(2,1)S(1)} %get-tuple-element.14), channel_id=1, source_target_pairs={{0,24},{4,28},{8,0},{12,4},{16,8},{20,12},{24,16},{28,20},{1,25},{... | collective-permute-start | bytes 49160 | tf_op jit(solution)/shard_map/ppermute | solution.py:270
  102.3 1.6 %collective-permute-start.6 = (bf16[16,4,128]{2,0,1:T(8,128)(2,1)S(1)}, bf16[16,4,128]{2,0,1:T(8,128)(2,1)S(1)}, u32[]{:S(2)}, u32[]{:S(2)}) collective-permute-start(bf16[16,4,128]{2,0,1:T(8,128)(2,1)S(1)} %get-tuple-element.13), channel_id=1, source_target_pairs={{0,28},{4,0},{8,4},{12,8},{16,12},{20,16},{24,20},{28,24},{1,29},{... | collective-permute-start | bytes 49160 | tf_op jit(solution)/shard_map/ppermute | solution.py:270
